TPU v7x, 32 devices: a whole 2x2x4 slice. The times are simulated.
32 devices in a mesh: batch: 8 (over z, x), phase: 2 (over core), mp: 2 (over y).
Axes of the slice: x: 2, y: 2, z: 4, core: 2. Of those that a mesh axis runs over, the one named last changes fastest.
Arguments:
- images: bfloat16 [64, 4, 4, 768], P('batch'), may hold values from -6 to 6
- conv_kernels: float32 [2, 7, 7, 768], P('phase'), may hold values from -0.875 to 0.875
- norm_gains: float32 [2, 768], P('phase'), may hold values from 0.1 to 1.9
- expand_weight: bfloat16 [2, 768, 3072], P('phase', None, 'mp'), may hold values from -0.21875 to 0.21875
- project_weight: bfloat16 [2, 3072, 768], P('phase', 'mp'), may hold values from -0.109375 to 0.109375
- head_weight: bfloat16 [768, 1024], replicated, may hold values from -0.21875 to 0.21875
- texts: bfloat16 [64, 1024], P('batch'), may hold values from -6 to 6
- pair_index: int32 [64], P('batch'), may hold values from 0 to 63
Outputs:
- input_grads: float32 [2, 64, 4, 4, 768], P('phase', 'batch')
Inputs may be any that keep to these rules, and one draw needn't show every extreme that they name: Image i and text pair_index[i] form a positive pair.
All inputs are finite; a program needn't handle non-finite values.
Results may differ from a plain program's by a relative error of at most 0.018.
Values may be sent and summed in bfloat16 or wider, within the bound.
No kernel may reach another device: no remote copies, remote signals or barrier semaphores. Data moves between devices by JAX's collectives and lax.ppermute only.
A program may use at most 64 MiB of HBM per device.

v0:
```python
import jax
import jax.numpy as jnp
import numpy as np
from jax import lax
from jax.sharding import PartitionSpec as P

inverse_softness_factor = 30.0


def swapped(value, axis, stride):
    return lax.ppermute(value, axis, [(i, i ^ 1 << stride) for i in range(lax.axis_size(axis))])


def depthwise(values, kernel):
    kernel_side = kernel.shape[0]
    margin = kernel_side // 2
    grid_side = values.shape[1]
    cells = np.arange(grid_side * grid_side)
    cell_row = cells // grid_side
    cell_col = cells % grid_side
    tap_row = np.clip(cell_row[None, :] - cell_row[:, None] + margin, 0, kernel_side - 1)
    tap_col = np.clip(cell_col[None, :] - cell_col[:, None] + margin, 0, kernel_side - 1)
    inside = (
        (np.abs(cell_row[None, :] - cell_row[:, None]) <= margin)
        & (np.abs(cell_col[None, :] - cell_col[:, None]) <= margin)
    ).astype(np.float32)
    operator = kernel[tap_row, tap_col] * jnp.asarray(inside, dtype=kernel.dtype)[:, :, None]
    flat = values.reshape(values.shape[0], grid_side * grid_side, values.shape[3])
    result = jnp.einsum("oic,bic->boc", operator, flat, precision=lax.Precision.HIGHEST)
    return result.reshape(values.shape)


def normalize_last(values):
    centred = values - jnp.mean(values, axis=-1, keepdims=True)
    variance = jnp.mean(centred * centred, axis=-1, keepdims=True)
    return centred * lax.rsqrt(variance + 1e-06)


def front_part(values, kernel, gain_vec):
    return normalize_last(depthwise(values, kernel)) * gain_vec


def mlp_part(normed, expand, project_out):
    flattened = normed.reshape(-1, normed.shape[-1]).astype(jnp.bfloat16)
    hidden = jax.nn.gelu(jnp.dot(flattened, expand, preferred_element_type=jnp.float32)).astype(
        jnp.bfloat16
    )
    return jnp.dot(hidden, project_out, preferred_element_type=jnp.float32).reshape(normed.shape)


def head_part(values, head_weight):
    pooled = jnp.mean(values, axis=(1, 2))
    normed = normalize_last(pooled).astype(jnp.bfloat16)
    embedded = jnp.dot(normed, head_weight, preferred_element_type=jnp.float32)
    return embedded * lax.rsqrt(jnp.sum(embedded * embedded, axis=-1, keepdims=True) + 1e-06)


def unit_text(texts):
    widened = texts.astype(jnp.float32)
    return (widened * lax.rsqrt(jnp.sum(widened * widened, axis=-1, keepdims=True) + 1e-06)).astype(
        jnp.bfloat16
    )


def hidden_total(values):
    return lax.psum(values.astype(jnp.bfloat16), "mp").astype(jnp.float32)


def hand_over(values):
    return swapped(values, "phase", 0)


def section_forward(inputs_low, kernel, gain_vec, expand, project_out):
    widened = inputs_low.astype(jnp.float32)
    normed, front_back = jax.vjp(lambda inner: front_part(inner, kernel, gain_vec), widened)
    partial_out, mlp_back = jax.vjp(lambda inner: mlp_part(inner, expand, project_out), normed)
    summed = hidden_total(partial_out)
    return ((widened + summed).astype(jnp.bfloat16), front_back, mlp_back)


def section_backward(cotangent, front_back, mlp_back):
    (partial_grad,) = mlp_back(cotangent)
    (from_front,) = front_back(hidden_total(partial_grad))
    return cotangent + from_front


def make_fold(vector_lowered_total, pair_index, row_map):

    def fold_texts(state_now, text_block, first_row):
        block_rows = text_block.shape[0]
        cosine_score_matrix = inverse_softness_factor * jnp.einsum(
            "ie,je->ij", vector_lowered_total, text_block, preferred_element_type=jnp.float32
        )
        weights = jnp.exp(cosine_score_matrix).astype(jnp.bfloat16)
        softmax_denominators = jnp.sum(weights.astype(jnp.float32), axis=1)
        softmax_scaled_captions = jnp.dot(weights, text_block, preferred_element_type=jnp.float32)
        global_rows = row_map(jnp.arange(block_rows, dtype=jnp.int32))
        onehot = (pair_index[:, None] == global_rows[None, :]).astype(jnp.bfloat16)
        diagonal_matched_scores = jnp.dot(onehot, text_block, preferred_element_type=jnp.float32)
        return (softmax_denominators, softmax_scaled_captions, diagonal_matched_scores)

    return fold_texts


def on_device(
    images, conv_kernels, norm_gains, expand_weight, project_weight, head_weight, texts, pair_index
):
    phase_pick = lax.axis_index("phase")
    kernel = conv_kernels[0]
    gain_vec = norm_gains[0]
    expand = expand_weight[0]
    project_out = project_weight[0]
    first_out, front_one, mlp_one = section_forward(images, kernel, gain_vec, expand, project_out)
    handed = hand_over(first_out)
    second_out, front_two, mlp_two = section_forward(handed, kernel, gain_vec, expand, project_out)
    embed, head_back = jax.vjp(
        lambda inner: head_part(inner, head_weight), second_out.astype(jnp.float32)
    )
    vector_lowered_total = embed.astype(jnp.bfloat16)
    caption_unit_vectors = unit_text(texts)
    image_rows = embed.shape[0]
    embed_width = embed.shape[1]
    text_rows = caption_unit_vectors.shape[0]
    share_count = 1
    share_rows = text_rows // share_count

    def share_map(rows_now):
        return rows_now // share_rows * text_rows + rows_now % share_rows

    start_state = (
        jnp.zeros((image_rows,), jnp.float32),
        jnp.zeros((image_rows, embed_width), jnp.float32),
        jnp.zeros((image_rows, embed_width), jnp.float32),
    )
    fold_texts = make_fold(vector_lowered_total, pair_index, share_map)
    softmax_denominators, softmax_scaled_captions, diagonal_matched_scores = fold_texts(
        start_state, lax.all_gather(caption_unit_vectors, "batch", axis=0, tiled=True), jnp.int32(0)
    )
    encoder_output_slope = inverse_softness_factor * (
        softmax_scaled_captions / softmax_denominators[:, None] - diagonal_matched_scores
    )
    (grad_second,) = head_back(encoder_output_slope)
    grad_first_in = section_backward(grad_second, front_two, mlp_two)
    returned = hand_over(grad_first_in.astype(jnp.bfloat16))
    grad_images = section_backward(returned.astype(jnp.float32), front_one, mlp_one)
    chosen = jnp.where(phase_pick == 0, grad_images, grad_first_in)
    return chosen[None]


def solution(mesh):
    return jax.shard_map(
        on_device,
        mesh=mesh,
        in_specs=(
            P("batch", None, None, None),
            P("phase", None, None, None),
            P("phase", None),
            P("phase", None, "mp"),
            P("phase", "mp", None),
            P(),
            P("batch", None),
            P("batch"),
        ),
        out_specs=P("phase", "batch", None, None, None),
        check_vma=False,
    )
```

profile of v0, /device:TPU:0, one launch (start us, length us, event | category | flops | bytes accessed | tf_op | source)
XLA Modules:
  0.0 215.0 jit_solution(14726889605407176546)
XLA Ops:
  6.5 1.1 copy.165
  7.6 1.0 reshape.232
  8.6 1.9 copy.122
  10.5 1.7 gather_fusion
  12.2 5.0 %copy.121 = f32[16,16,768]{1,0,2:T(8,128)} copy(f32[16,16,768]{2,1,0:T(8,128)S(1)} %bitcast.116) | data formatting | bytes 1572864 | tf_op jit(solution)/shard_map/jvp()/gather | solution.py:27
  17.2 9.9 %bitcast_reduce_fusion.1 = (f32[8,16]{1,0:T(8,128)S(1)}, f32[768,16,8]{1,2,0:T(8,128)}) fusion(f32[16,16,768]{1,0,2:T(8,128)} %copy.121, bf16[8,16,768]{1,0,2:T(8,128)(2,1)} %copy.122), kind=kOutput, calls=%fused_computation.161 | convolution fusion | flops 18972544 | bytes 1376768 | tf_op jit(solution)/shard_map/jvp(oic,bic->boc)/dot_general | solution.py:29
  27.1 2.3 %copy.123 = f32[768,16,8]{0,1,2:T(8,128)S(1)} copy(f32[768,16,8]{1,2,0:T(8,128)} %get-tuple-element.18) | data formatting | bytes 786432 | tf_op jit(solution)/shard_map/jvp(oic,bic->boc)/dot_general | solution.py:29
  29.8 1.5 multiply_convert_fusion.1
  31.4 3.0 %fusion.16 = bf16[8,4,4,768]{3,0,2,1:T(8,128)(2,1)} fusion(bf16[1,1536,768]{2,1,0:T(8,128)(2,1)} %param.22, bf16[8,4,4,1536]{3,2,1,0:T(4,128)(2,1)S(1)} %dot_general.57), kind=kOutput, calls=%fused_computation.21 | convolution fusion | flops 302088192 | bytes 2949120 | tf_op jit(solution)/shard_map/jvp()/dot_general | solution.py:48
  34.4 0.2 all-reduce.7.cloned.1.call-start
  34.8 25.0 %all-reduce.5.cloned.1.call-done = bf16[8,4,4,768]{3,0,2,1:T(8,128)(2,1)} async-done(((bf16[8,4,4,768]{3,0,2,1:T(8,128)(2,1)}), bf16[8,4,4,768]{3,0,2,1:T(8,128)(2,1)}) %all-reduce.5.cloned.1.call-update) | async-done | bytes 196624 | tf_op jit(solution)/shard_map/psum | solution.py:66
  59.8 1.0 add_convert_fusion.1
  60.9 1.4 collective-permute-done
  62.3 1.9 copy.127
  64.2 9.9 %bitcast_reduce_fusion = (f32[8,16]{1,0:T(8,128)S(1)}, f32[768,8,16]{2,1,0:T(8,128)}) fusion(bf16[8,16,768]{1,0,2:T(8,128)(2,1)} %copy.127, f32[16,16,768]{1,0,2:T(8,128)} %copy.121), kind=kOutput, calls=%fused_computation.160 | convolution fusion | flops 18972544 | bytes 1376768 | tf_op jit(solution)/shard_map/jvp(oic,bic->boc)/dot_general | solution.py:29
  74.0 2.3 %copy.129 = f32[768,8,16]{0,2,1:T(8,128)S(1)} copy(f32[768,8,16]{2,1,0:T(8,128)} %get-tuple-element.22) | data formatting | bytes 786432 | tf_op jit(solution)/shard_map/jvp(oic,bic->boc)/dot_general | solution.py:29
  76.7 1.5 multiply_convert_fusion
  78.3 3.0 %fusion.19 = bf16[8,4,4,768]{3,0,2,1:T(8,128)(2,1)} fusion(bf16[1,1536,768]{2,1,0:T(8,128)(2,1)} %param.22, bf16[8,4,4,1536]{3,2,1,0:T(4,128)(2,1)S(1)} %dot_general.61), kind=kOutput, calls=%fused_computation.22 | convolution fusion | flops 302088192 | bytes 2949120 | tf_op jit(solution)/shard_map/jvp()/dot_general | solution.py:48
  81.4 30.6 %all_gather.3 = bf16[64,1024]{1,0:T(8,128)(2,1)S(1)} all-gather(bf16[8,1024]{1,0:T(8,128)(2,1)S(1)} %fusion.94), channel_id=1, replica_groups=mesh['batch'=8,'phase'=2,'mp'=2] {'batch'}, dimensions={0}, use_global_device_ids=true | all-gather | bytes 147456 | tf_op jit(solution)/shard_map/all_gather | solution.py:137
  112.0 1.1 convert_reduce_fusion
  113.4 1.9 multiply_reduce_fusion.5
  115.3 0.3 convert_reduce_fusion.1
  115.8 0.3 multiply_reduce_fusion.4
  116.1 0.6 multiply_reduce_fusion.6
  117.2 3.6 %fusion.22 = bf16[128,768]{1,0:T(8,128)(2,1)S(1)} fusion(bf16[1,768,1536]{2,1,0:T(8,128)(2,1)S(1)} %copy-done, f32[128,1536]{1,0:T(8,128)} %get-tuple-element.24, bf16[128,768]{1,0:T(8,128)(2,1)S(1)} %reshape.234, bf16[1,1536,768]{2,1,0:T(8,128)(2,1)} %param.22), kind=kOutput, calls=%fused_computation.23 | convolution fusion | flops 608108544 | bytes 5898240 | tf_op jit(solution)/shard_map/transpose(jvp())/dot_general | solution.py:45
  120.8 0.7 copy.134
  121.6 0.3 all-reduce.11.cloned.1.call-start
  121.9 2.4 %copy.136 = f32[8,16,768]{2,0,1:T(8,128)S(1)} copy(f32[8,16,768]{1,0,2:T(8,128)} %bitcast.109) | data formatting | bytes 786432 | tf_op jit(solution)/shard_map/jvp(oic,bic->boc)/transpose | solution.py:29
  124.4 19.8 %all-reduce.9.cloned.1.call-done = bf16[8,4,4,768]{3,0,2,1:T(8,128)(2,1)} async-done(((bf16[8,4,4,768]{3,0,2,1:T(8,128)(2,1)}), bf16[8,4,4,768]{3,0,2,1:T(8,128)(2,1)}) %all-reduce.9.cloned.1.call-update) | async-done | bytes 196624 | tf_op jit(solution)/shard_map/psum | solution.py:66
  144.1 1.1 multiply_reduce_fusion.1
  145.3 1.2 fusion.91
  146.4 1.1 broadcast_add_fusion.1
  147.5 2.2 %copy.138 = f32[768,8,16]{2,1,0:T(8,128)} copy(f32[768,8,16]{0,1,2:T(8,128)S(1)} %bitcast.118) | data formatting | bytes 786432 | tf_op jit(solution)/shard_map/transpose(jvp(oic,bic->boc))/transpose | solution.py:29
  149.7 9.1 %convolution_bitcast_fusion.1 = f32[8,16,768]{1,0,2:T(8,128)} fusion(f32[768,8,16]{2,1,0:T(8,128)} %copy.138, f32[16,16,768]{1,0,2:T(8,128)} %copy.121), kind=kOutput, calls=%fused_computation.20 | convolution fusion | flops 18874368 | bytes 1572864 | tf_op jit(solution)/shard_map/transpose(jvp(oic,bic->boc))/dot_general | solution.py:29
  158.7 2.4 %copy.140 = f32[8,16,768]{2,0,1:T(8,128)S(1)} copy(f32[8,16,768]{1,0,2:T(8,128)} %convolution_bitcast_fusion.1) | data formatting | bytes 786432 | tf_op jit(solution)/shard_map/transpose(jvp(oic,bic->boc))/transpose | solution.py:29
  161.2 1.4 collective-permute-done.1
  162.7 0.7 copy-done.3
  163.5 3.5 %fusion.25 = bf16[128,768]{1,0:T(8,128)(2,1)S(1)} fusion(bf16[1,768,1536]{2,1,0:T(8,128)(2,1)S(1)} %copy-done, f32[128,1536]{1,0:T(8,128)} %get-tuple-element.20, bf16[128,768]{1,0:T(8,128)(2,1)S(1)} %reshape.238, bf16[1,1536,768]{2,1,0:T(8,128)(2,1)} %param.22), kind=kOutput, calls=%fused_computation.24 | convolution fusion | flops 608206848 | bytes 5898240 | tf_op jit(solution)/shard_map/transpose(jvp())/dot_general | solution.py:45
  167.1 0.7 copy.142
  167.9 2.4 %copy.144 = f32[8,16,768]{2,0,1:T(8,128)S(1)} copy(f32[8,16,768]{1,0,2:T(8,128)} %bitcast.108) | data formatting | bytes 786432 | tf_op jit(solution)/shard_map/jvp(oic,bic->boc)/transpose | solution.py:29
  170.4 20.0 %all-reduce.11.cloned.1.call-done = bf16[8,4,4,768]{3,0,2,1:T(8,128)(2,1)} async-done(((bf16[8,4,4,768]{3,0,2,1:T(8,128)(2,1)}), bf16[8,4,4,768]{3,0,2,1:T(8,128)(2,1)}) %all-reduce.11.cloned.1.call-update) | async-done | bytes 196624 | tf_op jit(solution)/shard_map/psum | solution.py:66
  190.4 1.1 multiply_reduce_fusion
  191.5 1.2 fusion.92
  192.7 1.1 broadcast_add_fusion
  193.8 2.3 %copy.146 = f32[768,8,16]{2,1,0:T(8,128)} copy(f32[768,8,16]{0,1,2:T(8,128)S(1)} %bitcast.117) | data formatting | bytes 786432 | tf_op jit(solution)/shard_map/transpose(jvp(oic,bic->boc))/transpose | solution.py:29
  196.1 9.1 %convolution_bitcast_fusion = f32[8,16,768]{1,0,2:T(8,128)} fusion(f32[768,8,16]{2,1,0:T(8,128)} %copy.146, f32[16,16,768]{1,0,2:T(8,128)} %copy.121), kind=kOutput, calls=%fused_computation.19 | convolution fusion | flops 18874368 | bytes 1572864 | tf_op jit(solution)/shard_map/transpose(jvp(oic,bic->boc))/dot_general | solution.py:29
  205.1 2.4 %copy.148 = f32[8,16,768]{2,0,1:T(8,128)S(1)} copy(f32[8,16,768]{1,0,2:T(8,128)} %convolution_bitcast_fusion) | data formatting | bytes 786432 | tf_op jit(solution)/shard_map/transpose(jvp(oic,bic->boc))/transpose | solution.py:29
  207.6 0.9 copy.149
  (72 shorter events, 2.9 us)
Async XLA Ops:
  6.5 23.3 %copy-start = (bf16[1,768,1536]{2,1,0:T(8,128)(2,1)S(1)}, bf16[1,768,1536]{2,1,0:T(8,128)(2,1)}, u32[]{:S(2)}) copy-start(bf16[1,768,1536]{2,1,0:T(8,128)(2,1)} %param.21) | copy-start | bytes 7077892
  6.5 3.9 %copy-start.1 = (s32[256]{0:T(256)S(1)}, s32[256]{0:T(256)}, u32[]{:S(2)}) copy-start(s32[256]{0:T(256)} %constant.120) | copy-start | bytes 3076
  6.5 53.2 %all-reduce.5.cloned.1.call-start = ((), (), s32[]{:S(2)}) async-start(), calls=%async_computation | async-start | bytes 393216 | tf_op jit(solution)/shard_map/psum | solution.py:66
  27.1 2.5 %copy-start.9 = (f32[1,768]{1,0:T(1,128)S(1)}, f32[1,768]{1,0:T(1,128)}, u32[]{:S(2)}) copy-start(f32[1,768]{1,0:T(1,128)} %param.20) | copy-start | bytes 9220
  31.4 3.3 %copy-start.8 = (bf16[8,1024]{1,0:T(8,128)(2,1)S(1)}, bf16[8,1024]{1,0:T(8,128)(2,1)}, u32[]{:S(2)}) copy-start(bf16[8,1024]{1,0:T(8,128)(2,1)} %param.24) | copy-start | bytes 49156
  31.4 28.4 %copy-start.5 = (bf16[8,4,4,768]{3,2,1,0:T(4,128)(2,1)S(1)}, bf16[8,4,4,768]{3,2,1,0:T(4,128)(2,1)}, u32[]{:S(2)}) copy-start(bf16[8,4,4,768]{3,2,1,0:T(4,128)(2,1)} %param.18) | copy-start | bytes 589828
  34.4 77.6 %all-reduce.7.cloned.1.call-start = ((), (), s32[]{:S(2)}) async-start(), calls=%async_computation.1 | async-start | bytes 393216 | tf_op jit(solution)/shard_map/psum | solution.py:66
  60.8 1.5 collective-permute-start
  81.3 34.5 %copy-start.10 = (s32[8]{0:T(128)S(1)}, s32[8]{0:T(128)}, u32[]{:S(2)}) copy-start(s32[8]{0:T(128)} %param.25) | copy-start | bytes 100
  81.3 62.8 %all-reduce.9.cloned.1.call-start = ((), (), s32[]{:S(2)}) async-start(), calls=%async_computation.2 | async-start | bytes 393216 | tf_op jit(solution)/shard_map/psum | solution.py:66
  112.0 4.1 %copy-start.2 = (bf16[768,1024]{1,0:T(8,128)(2,1)S(1)}, bf16[768,1024]{1,0:T(8,128)(2,1)}, u32[]{:S(2)}) copy-start(bf16[768,1024]{1,0:T(8,128)(2,1)} %param.23) | copy-start | bytes 4718596
  117.1 44.0 %copy-start.6 = (f32[8,768]{1,0:T(8,128)}, f32[8,768]{1,0:T(8,128)S(1)}, u32[]{:S(2)}) copy-start(f32[8,768]{1,0:T(8,128)S(1)} %add_multiply_fusion) | copy-start | bytes 73732
  121.6 68.8 %all-reduce.11.cloned.1.call-start = ((), (), s32[]{:S(2)}) async-start(), calls=%async_computation.3 | async-start | bytes 393216 | tf_op jit(solution)/shard_map/psum | solution.py:66
  161.1 1.5 collective-permute-start.1
  162.7 0.7 copy-start.3
  205.1 2.4 %copy-start.4 = (bf16[8,4,4,768]{3,0,2,1:T(8,128)(2,1)S(1)}, bf16[8,4,4,768]{3,0,2,1:T(8,128)(2,1)}, u32[]{:S(2)}) copy-start(bf16[8,4,4,768]{3,0,2,1:T(8,128)(2,1)} %copy-done.3) | copy-start | bytes 589828
  205.1 2.4 %copy-start.7 = (f32[8,768]{1,0:T(8,128)S(1)}, f32[8,768]{1,0:T(8,128)}, u32[]{:S(2)}) copy-start(f32[8,768]{1,0:T(8,128)} %copy-done.6) | copy-start | bytes 73732
Sparse Core Ops, SparseCore 0:
  34.5 25.1 all-reduce.4
  81.4 22.3 all-reduce.6
  121.7 22.3 all-reduce.8
  168.0 22.3 all-reduce.10
where the time goes:
time: 216 us; the launch traced here: 215 us
  waiting for transfers between devices  67.7 us (31%)
  matrix products  57.2 us (26%)
  local copies, waits for them, and re-layouts  34.9 us (16%)
  blocking collectives  30.6 us (14%)
  between operations  13.5 us (6%)
  other arithmetic  10.5 us (5%)
    psum x4, waiting for transfers between devices, hidden_total(): return lax.psum(values.astype(jnp.bfloat16), 'mp').astype(jnp.float32)  64.8 us
    dot_general x4, matrix products, depthwise(): jnp.einsum('oic,bic->boc', operator, flat, precision=lax.Precision.HIGHEST)  37.9 us
    all_gather x1, blocking collectives, on_device(): lax.all_gather(caption_unit_vectors, 'batch', axis=0, tiled=True)  30.6 us
    transpose x6, local copies, waits for them, and re-layouts, depthwise(): jnp.einsum('oic,bic->boc', operator, flat, precision=lax.Precision.HIGHEST)  13.9 us
    dot_general x4, matrix products, mlp_part(): jnp.dot(flattened, expand, preferred_element_type=jnp.float32)  10.1 us
    gather x2, local copies, waits for them, and re-layouts, depthwise(): kernel[tap_row, tap_col]  6.7 us
    dot_general x2, matrix products, mlp_part(): jnp.dot(hidden, project_out, preferred_element_type=jnp.float32)  5.97 us
    reshape x3, local copies, waits for them, and re-layouts, depthwise(): values.reshape(values.shape[0], grid_side * grid_side, values.shape[3])  4.71 us
  transfers between devices with their start and end apart: 6, of which 5 were waited for; matrix products, arithmetic and copies ran while one was open for 2% of the time, Pallas kernels for 0%

commit v1 on v0

--- a/solution.py
+++ b/solution.py
@@ -63,7 +63,9 @@
 
 
 def hidden_total(values):
-    return lax.psum(values.astype(jnp.bfloat16), "mp").astype(jnp.float32)
+    return jnp.sum(jax.lax.all_gather(values.astype(jnp.bfloat16), axis_name="mp"), axis=0).astype(
+        jnp.float32
+    )
 
 
 def hand_over(values):

time: 216 us -> 162 us (0.75)
  waiting for transfers between devices: 67.7 us -> 1.42 us
  blocking collectives: 30.6 us -> 60.4 us
  between operations: 13.5 us -> 0.47 us
  local copies, waits for them, and re-layouts: 34.9 us -> 32.1 us
    psum x4 -> x0, waiting for transfers between devices: 64.8 us -> none  [hidden_total(): return lax.psum(values.astype(jnp.bfloat16), 'mp').astype(jnp.float32)]
    all_gather x0 -> x4, blocking collectives: none -> 29.1 us  [hidden_total(): jax.lax.all_gather(values.astype(jnp.bfloat16), axis_name='mp')]
    transpose x6 -> x4, local copies, waits for them, and re-layouts: 13.9 us -> 9.25 us  [depthwise(): jnp.einsum('oic,bic->boc', operator, flat, precision=lax.Precision.HIGHEST)]
    add_any x2 -> x0, other arithmetic: 2.17 us -> none  [normalize_last(): centred = values - jnp.mean(values, axis=-1, keepdims=True)]
  transfers between devices with their start and end apart: 6 -> 2, of which waited for: 5 -> 1; matrix products, arithmetic and copies ran while one was open for 2% -> 0% of each run, Pallas kernels for 0% -> 0%
where the time goes in v1:
time: 162 us; the launch traced here: 161 us
  blocking collectives  60.4 us (37%)
  matrix products  56.3 us (35%)
  local copies, waits for them, and re-layouts  32.1 us (20%)
  other arithmetic  10.3 us (6%)
    dot_general x4, matrix products, depthwise(): jnp.einsum('oic,bic->boc', operator, flat, precision=lax.Precision.HIGHEST)  38 us
    all_gather x1, blocking collectives, on_device(): lax.all_gather(caption_unit_vectors, 'batch', axis=0, tiled=True)  31.3 us
    all_gather x4, blocking collectives, hidden_total(): jax.lax.all_gather(values.astype(jnp.bfloat16), axis_name='mp')  29.1 us
    dot_general x4, matrix products, mlp_part(): jnp.dot(flattened, expand, preferred_element_type=jnp.float32)  11.6 us
    transpose x4, local copies, waits for them, and re-layouts, depthwise(): jnp.einsum('oic,bic->boc', operator, flat, precision=lax.Precision.HIGHEST)  9.25 us
    gather x2, local copies, waits for them, and re-layouts, depthwise(): kernel[tap_row, tap_col]  6.84 us
    dot_general x2, matrix products, mlp_part(): jnp.dot(hidden, project_out, preferred_element_type=jnp.float32)  4.84 us
    dot_general x2, local copies, waits for them, and re-layouts, depthwise(): jnp.einsum('oic,bic->boc', operator, flat, precision=lax.Precision.HIGHEST)  4.64 us
  transfers between devices with their start and end apart: 2, of which 1 were waited for; matrix products, arithmetic and copies ran while one was open for 0% of the time, Pallas kernels for 0%

profile of v1, /device:TPU:0, one launch (start us, length us, event | category | flops | bytes accessed | tf_op | source)
XLA Modules:
  0.0 161.1 jit_solution(7638159513696866442)
XLA Ops:
  0.0 1.1 copy.142
  1.1 1.8 %gather_fusion = f32[256,768]{1,0:T(8,128)S(1)} fusion(f32[7,7,768]{2,1,0:T(8,128)S(1)} %bitcast.117, s32[256]{0:T(256)} %constant.125), kind=kCustom, calls=%fused_computation | custom fusion | bytes 1574912 | tf_op jit(solution)/shard_map/jvp()/gather | solution.py:27
  3.0 5.0 %copy.88 = f32[16,16,768]{1,0,2:T(8,128)} copy(f32[16,16,768]{2,1,0:T(8,128)S(1)} %bitcast.120) | data formatting | bytes 1572864 | tf_op jit(solution)/shard_map/jvp()/gather | solution.py:27
  8.0 1.9 %copy.89 = bf16[8,16,768]{1,0,2:T(8,128)(2,1)} copy(bf16[8,16,768]{2,1,0:T(8,128)(2,1)S(1)} %reshape.268) | data formatting | bytes 393216 | tf_op jit(solution)/shard_map/jvp()/reshape | solution.py:28
  9.9 9.9 %fusion.126 = f32[768,16,8]{1,2,0:T(8,128)} fusion(f32[16,16,768]{1,0,2:T(8,128)} %copy.88, bf16[8,16,768]{1,0,2:T(8,128)(2,1)} %copy.89), kind=kOutput, calls=%fused_computation.180 | convolution fusion | flops 18874368 | bytes 1376256 | tf_op jit(solution)/shard_map/jvp(oic,bic->boc)/dot_general | solution.py:29
  19.8 2.3 %copy.90 = f32[768,16,8]{0,1,2:T(8,128)S(1)} copy(f32[768,16,8]{1,2,0:T(8,128)} %fusion.126) | data formatting | bytes 786432 | tf_op jit(solution)/shard_map/jvp(oic,bic->boc)/dot_general | solution.py:29
  22.6 1.5 multiply_convert_fusion.1
  24.2 2.3 %fusion.16 = bf16[8,4,4,768]{3,0,2,1:T(8,128)(2,1)S(1)} fusion(bf16[1,1536,768]{2,1,0:T(8,128)(2,1)} %param.22, bf16[8,4,4,1536]{3,2,1,0:T(4,128)(2,1)S(1)} %dot_general.57), kind=kOutput, calls=%fused_computation.21 | convolution fusion | flops 302088192 | bytes 2949120 | tf_op jit(solution)/shard_map/jvp()/dot_general | solution.py:48
  26.6 8.6 %all-gather = bf16[16,4,4,768]{3,0,2,1:T(8,128)(2,1)S(1)} all-gather(bf16[8,4,4,768]{3,0,2,1:T(8,128)(2,1)S(1)} %fusion.16), channel_id=2, replica_groups=mesh['batch'=8,'phase'=2,'mp'=2] {'mp'}, dimensions={0}, use_global_device_ids=true | all-gather | bytes 589824 | tf_op jit(solution)/shard_map/all_gather | solution.py:66
  35.6 31.3 %all_gather.27 = bf16[64,1024]{1,0:T(8,128)(2,1)S(1)} all-gather(bf16[8,1024]{1,0:T(8,128)(2,1)S(1)} %fusion.92), channel_id=1, replica_groups=mesh['batch'=8,'phase'=2,'mp'=2] {'batch'}, dimensions={0}, use_global_device_ids=true | all-gather | bytes 147456 | tf_op jit(solution)/shard_map/all_gather | solution.py:139
  66.9 0.6 fusion.109
  67.4 1.9 %copy.92 = bf16[8,16,768]{1,0,2:T(8,128)(2,1)} copy(bf16[8,16,768]{2,0,1:T(8,128)(2,1)S(1)} %bitcast.122) | data formatting | bytes 393216 | tf_op jit(solution)/shard_map/jvp()/reshape | solution.py:28
  69.4 10.0 %fusion.127 = f32[768,8,16]{2,1,0:T(8,128)} fusion(bf16[8,16,768]{1,0,2:T(8,128)(2,1)} %copy.92, f32[16,16,768]{1,0,2:T(8,128)} %copy.88), kind=kOutput, calls=%fused_computation.181 | convolution fusion | flops 18874368 | bytes 1376256 | tf_op jit(solution)/shard_map/jvp(oic,bic->boc)/dot_general | solution.py:29
  79.3 2.3 %copy.94 = f32[768,8,16]{0,2,1:T(8,128)S(1)} copy(f32[768,8,16]{2,1,0:T(8,128)} %fusion.127) | data formatting | bytes 786432 | tf_op jit(solution)/shard_map/jvp(oic,bic->boc)/dot_general | solution.py:29
  82.1 1.6 multiply_convert_fusion
  83.7 1.8 %dot_general.61 = bf16[8,4,4,1536]{3,2,1,0:T(4,128)(2,1)} reshape(bf16[128,1536]{1,0:T(8,128)(2,1)} %get-tuple-element.11) | data formatting | bytes 786432 | tf_op jit(solution)/shard_map/jvp()/dot_general | solution.py:48
  85.5 2.5 %fusion.19 = bf16[8,4,4,768]{3,0,2,1:T(8,128)(2,1)S(1)} fusion(bf16[1,1536,768]{2,1,0:T(8,128)(2,1)} %param.22, bf16[8,4,4,1536]{3,2,1,0:T(4,128)(2,1)} %dot_general.61), kind=kOutput, calls=%fused_computation.22 | convolution fusion | flops 302088192 | bytes 2949120 | tf_op jit(solution)/shard_map/jvp()/dot_general | solution.py:48
  88.1 6.3 %all-gather.1 = bf16[16,4,4,768]{3,0,2,1:T(8,128)(2,1)S(1)} all-gather(bf16[8,4,4,768]{3,0,2,1:T(8,128)(2,1)S(1)} %fusion.19), channel_id=3, replica_groups=mesh['batch'=8,'phase'=2,'mp'=2] {'mp'}, dimensions={0}, use_global_device_ids=true | all-gather | bytes 589824 | tf_op jit(solution)/shard_map/all_gather | solution.py:66
  94.9 0.5 multiply_reduce_fusion.5
  95.3 0.3 convert_reduce_fusion.1
  95.8 0.3 multiply_reduce_fusion.4
  96.1 0.6 multiply_reduce_fusion.6
  97.1 0.6 copy-done.6
  97.8 4.2 %fusion.22 = bf16[128,768]{1,0:T(8,128)(2,1)} fusion(bf16[1,768,1536]{2,1,0:T(8,128)(2,1)S(1)} %copy-done, f32[128,1536]{1,0:T(8,128)} %get-tuple-element.12, bf16[128,768]{1,0:T(8,128)(2,1)S(1)} %reshape.270, bf16[1,1536,768]{2,1,0:T(8,128)(2,1)} %param.22), kind=kOutput, calls=%fused_computation.23 | convolution fusion | flops 608108544 | bytes 5898240 | tf_op jit(solution)/shard_map/transpose(jvp())/dot_general | solution.py:45
  102.0 1.0 convert_element_type.170
  103.1 6.6 %all_gather.28 = bf16[2,8,4,4,768]{4,1,3,2,0:T(8,128)(2,1)S(1)} all-gather(bf16[1,8,4,4,768]{4,1,3,2,0:T(8,128)(2,1)S(1)} %copy.97), channel_id=1, replica_groups=mesh['batch'=8,'phase'=2,'mp'=2] {'mp'}, dimensions={0}, use_global_device_ids=true | all-gather | bytes 589824 | tf_op jit(solution)/shard_map/all_gather | solution.py:66
  109.7 0.8 reduce_sum.244
  110.4 1.0 convert.6
  111.6 0.7 multiply_multiply_fusion.5
  112.3 1.0 fusion.95
  113.3 0.9 add_bitcast_fusion.1
  114.2 2.3 %copy.101 = f32[768,8,16]{2,1,0:T(8,128)} copy(f32[768,8,16]{0,2,1:T(8,128)S(1)} %add_bitcast_fusion.1) | data formatting | bytes 786432 | tf_op jit(solution)/shard_map/transpose(jvp(oic,bic->boc))/transpose | solution.py:29
  116.5 9.1 %convolution_bitcast_fusion.1 = f32[8,16,768]{1,0,2:T(8,128)} fusion(f32[768,8,16]{2,1,0:T(8,128)} %copy.101, f32[16,16,768]{1,0,2:T(8,128)} %copy.88), kind=kOutput, calls=%fused_computation.20 | convolution fusion | flops 18874368 | bytes 1572864 | tf_op jit(solution)/shard_map/transpose(jvp(oic,bic->boc))/dot_general | solution.py:29
  125.5 2.4 %copy.103 = f32[8,16,768]{2,0,1:T(8,128)S(1)} copy(f32[8,16,768]{1,0,2:T(8,128)} %convolution_bitcast_fusion.1) | data formatting | bytes 786432 | tf_op jit(solution)/shard_map/transpose(jvp(oic,bic->boc))/transpose | solution.py:29
  128.0 1.4 collective-permute-done.1
  129.5 0.7 reshape.272
  130.3 4.3 %fusion.25 = bf16[128,768]{1,0:T(8,128)(2,1)} fusion(bf16[1,768,1536]{2,1,0:T(8,128)(2,1)S(1)} %copy-done, f32[128,1536]{1,0:T(8,128)} %get-tuple-element.10, bf16[128,768]{1,0:T(8,128)(2,1)} %reshape.272, bf16[1,1536,768]{2,1,0:T(8,128)(2,1)} %param.22), kind=kOutput, calls=%fused_computation.24 | convolution fusion | flops 608206848 | bytes 5898240 | tf_op jit(solution)/shard_map/transpose(jvp())/dot_general | solution.py:45
  134.6 1.0 convert_element_type.178
  135.6 7.6 %all_gather.29 = bf16[2,8,4,4,768]{4,1,3,2,0:T(8,128)(2,1)S(1)} all-gather(bf16[1,8,4,4,768]{4,1,3,2,0:T(8,128)(2,1)S(1)} %copy.105), channel_id=1, replica_groups=mesh['batch'=8,'phase'=2,'mp'=2] {'mp'}, dimensions={0}, use_global_device_ids=true | all-gather | bytes 589824 | tf_op jit(solution)/shard_map/all_gather | solution.py:66
  143.2 0.8 reduce_sum.247
  144.0 1.0 convert.7
  145.2 0.7 multiply_multiply_fusion.4
  145.9 0.3 fusion.96
  146.2 0.2 add_bitcast_fusion
  146.4 2.3 %copy.109 = f32[768,8,16]{2,1,0:T(8,128)} copy(f32[768,8,16]{0,2,1:T(8,128)S(1)} %add_bitcast_fusion) | data formatting | bytes 786432 | tf_op jit(solution)/shard_map/transpose(jvp(oic,bic->boc))/transpose | solution.py:29
  148.7 9.1 %convolution_bitcast_fusion = f32[8,16,768]{1,0,2:T(8,128)} fusion(f32[768,8,16]{2,1,0:T(8,128)} %copy.109, f32[16,16,768]{1,0,2:T(8,128)} %copy.88), kind=kOutput, calls=%fused_computation.19 | convolution fusion | flops 18874368 | bytes 1572864 | tf_op jit(solution)/shard_map/transpose(jvp(oic,bic->boc))/dot_general | solution.py:29
  157.7 2.4 %copy.111 = f32[8,16,768]{2,0,1:T(8,128)S(1)} copy(f32[8,16,768]{1,0,2:T(8,128)} %convolution_bitcast_fusion) | data formatting | bytes 786432 | tf_op jit(solution)/shard_map/transpose(jvp(oic,bic->boc))/transpose | solution.py:29
  160.2 0.9 copy.112
  (76 shorter events, 3.3 us)
Async XLA Ops:
  0.0 22.6 %copy-start = (bf16[1,768,1536]{2,1,0:T(8,128)(2,1)S(1)}, bf16[1,768,1536]{2,1,0:T(8,128)(2,1)}, u32[]{:S(2)}) copy-start(bf16[1,768,1536]{2,1,0:T(8,128)(2,1)} %param.21) | copy-start | bytes 7077892
  2.9 5.0 %copy-start.4 = (bf16[8,4,4,768]{3,2,1,0:T(4,128)(2,1)S(1)}, bf16[8,4,4,768]{3,2,1,0:T(4,128)(2,1)}, u32[]{:S(2)}) copy-start(bf16[8,4,4,768]{3,2,1,0:T(4,128)(2,1)} %param.18) | copy-start | bytes 589828
  19.8 2.7 %copy-start.13 = (f32[1,768]{1,0:T(1,128)S(1)}, f32[1,768]{1,0:T(1,128)}, u32[]{:S(2)}) copy-start(f32[1,768]{1,0:T(1,128)} %param.20) | copy-start | bytes 9220
  22.4 1.8 %copy-start.11 = (f32[8,16]{1,0:T(8,128)}, f32[8,16]{1,0:T(8,128)S(1)}, u32[]{:S(2)}) copy-start(f32[8,16]{1,0:T(8,128)S(1)} %multiply_reduce_fusion.3) | copy-start | bytes 1540
  24.2 11.0 %copy-start.5 = (bf16[8,4,4,768]{3,2,1,0:T(4,128)(2,1)S(1)}, bf16[8,4,4,768]{3,2,1,0:T(4,128)(2,1)}, u32[]{:S(2)}) copy-start(bf16[8,4,4,768]{3,2,1,0:T(4,128)(2,1)} %param.18) | copy-start | bytes 589828
  24.2 11.1 %copy-start.10 = (bf16[8,1024]{1,0:T(8,128)(2,1)S(1)}, bf16[8,1024]{1,0:T(8,128)(2,1)}, u32[]{:S(2)}) copy-start(bf16[8,1024]{1,0:T(8,128)(2,1)} %param.24) | copy-start | bytes 49156
  35.3 32.2 %collective-permute-start = (bf16[8,4,4,768]{3,0,2,1:T(8,128)(2,1)S(1)}, bf16[8,4,4,768]{3,0,2,1:T(8,128)(2,1)S(1)}, u32[]{:S(2)}, u32[]{:S(2)}) collective-permute-start(bf16[8,4,4,768]{3,0,2,1:T(8,128)(2,1)S(1)} %add_convert_fusion.1), channel_id=1, source_target_pairs={{0,2},{2,0},{1,3},{3,1},{4,6},{6,4},{5,7},{7,5},{8,10},{10,8},{9,1... | collective-permute-start | bytes 589832 | tf_op jit(solution)/shard_map/ppermute | solution.py:11
  81.9 3.6 %copy-start.12 = (f32[8,16]{1,0:T(8,128)}, f32[8,16]{1,0:T(8,128)S(1)}, u32[]{:S(2)}) copy-start(f32[8,16]{1,0:T(8,128)S(1)} %multiply_reduce_fusion.2) | copy-start | bytes 1540
  82.0 3.6 %copy-start.9 = (f32[8,16]{1,0:T(8,128)}, f32[8,16]{1,0:T(8,128)S(1)}, u32[]{:S(2)}) copy-start(f32[8,16]{1,0:T(8,128)S(1)} %fusion.106) | copy-start | bytes 1540
  85.5 9.3 %copy-start.1 = (bf16[768,1024]{1,0:T(8,128)(2,1)S(1)}, bf16[768,1024]{1,0:T(8,128)(2,1)}, u32[]{:S(2)}) copy-start(bf16[768,1024]{1,0:T(8,128)(2,1)} %param.23) | copy-start | bytes 4718596
  88.1 7.8 %copy-start.14 = (s32[8]{0:T(128)S(1)}, s32[8]{0:T(128)}, u32[]{:S(2)}) copy-start(s32[8]{0:T(128)} %param.25) | copy-start | bytes 100
  88.1 7.7 %copy-start.15 = (s32[64]{0:T(128)S(1)}, s32[64]{0:T(128)}, u32[]{:S(2)}) copy-start(s32[64]{0:T(128)} %fusion.109) | copy-start | bytes 772
  97.1 0.6 copy-start.6
  125.5 2.4 %copy-start.7 = (f32[8,768]{1,0:T(8,128)S(1)}, f32[8,768]{1,0:T(8,128)}, u32[]{:S(2)}) copy-start(f32[8,768]{1,0:T(8,128)} %copy-done.6) | copy-start | bytes 73732
  128.0 1.5 collective-permute-start.1
  129.5 5.1 %copy-start.2 = (bf16[8,4,4,768]{3,0,2,1:T(8,128)(2,1)}, bf16[8,4,4,768]{3,0,2,1:T(8,128)(2,1)S(1)}, u32[]{:S(2)}) copy-start(bf16[8,4,4,768]{3,0,2,1:T(8,128)(2,1)S(1)} %collective-permute-done.1) | copy-start | bytes 589828
  157.7 2.4 %copy-start.3 = (bf16[8,4,4,768]{3,0,2,1:T(8,128)(2,1)S(1)}, bf16[8,4,4,768]{3,0,2,1:T(8,128)(2,1)}, u32[]{:S(2)}) copy-start(bf16[8,4,4,768]{3,0,2,1:T(8,128)(2,1)} %copy-done.2) | copy-start | bytes 589828
  157.7 2.4 %copy-start.8 = (f32[8,768]{1,0:T(8,128)S(1)}, f32[8,768]{1,0:T(8,128)}, u32[]{:S(2)}) copy-start(f32[8,768]{1,0:T(8,128)} %copy-done.6) | copy-start | bytes 73732
